TPU v7x, 256 devices: a whole 4x4x8 slice. The times are simulated.
256 devices in a mesh: hid: 32 (over z_hi, x, core), wid: 8 (over z_lo, y).
Axes of the slice: x: 4, y: 4, z: 8 (z_hi: 4, z_lo: 2; z = z_hi * 2 + z_lo), core: 2. Of those that a mesh axis runs over, the one named last changes fastest.
Arguments:
- inputs: bfloat16 [768, 8192], P('hid', 'wid'), may hold values from -6 to 6
- gate_weight: bfloat16 [8192, 28672], P('wid', 'hid'), may hold values from -0.0625 to 0.0625
- up_weight: bfloat16 [8192, 28672], P('wid', 'hid'), may hold values from -0.0625 to 0.0625
- down_weight: bfloat16 [28672, 8192], P('hid', 'wid'), may hold values from -0.03125 to 0.03125
- out_grad: bfloat16 [768, 8192], P('hid', 'wid'), may hold values from -0.43164062 to 0.43164062
Outputs:
- input_grad: bfloat16 [768, 8192], P('hid', 'wid')
- gate_grad: bfloat16 [8192, 28672], P('wid', 'hid')
- up_grad: bfloat16 [8192, 28672], P('wid', 'hid')
- down_grad: bfloat16 [28672, 8192], P('hid', 'wid')
All inputs are finite; a program needn't handle non-finite values.
Results may differ from a plain program's by a relative error of at most 0.02.
Values may be sent and summed in bfloat16 or wider, within the bound.
No kernel may reach another device: no remote copies, remote signals or barrier semaphores. Data moves between devices by JAX's collectives and lax.ppermute only.
A program may use at most 64 MiB of HBM per device.

v0:
```python
import jax
import jax.numpy as jnp
from jax import lax
from jax.sharding import PartitionSpec as P


def swiglu_terms(gate, up, hidden_grad):
    sigma = jax.nn.sigmoid(gate)
    hidden = (gate * sigma * up).astype(jnp.bfloat16)
    up_term = (hidden_grad * gate * sigma).astype(jnp.bfloat16)
    gate_term = (hidden_grad * up * sigma * (1.0 + gate * (1.0 - sigma))).astype(jnp.bfloat16)
    return (hidden, gate_term, up_term)


def per_device(inputs, gate_weight, up_weight, down_weight, out_grad):
    all_inputs, all_grads = (
        lax.all_gather(inputs, "hid", axis=0, tiled=True),
        lax.all_gather(out_grad, "hid", axis=0, tiled=True),
    )
    contract_last = (((1,), (1,)), ((), ()))
    gate_part = jnp.dot(all_inputs, gate_weight, preferred_element_type=jnp.float32)
    up_part = jnp.dot(all_inputs, up_weight, preferred_element_type=jnp.float32)
    grad_part = lax.dot_general(
        all_grads, down_weight, contract_last, preferred_element_type=jnp.float32
    )
    gate, up, hidden_grad = (
        lax.psum(gate_part.astype(jnp.bfloat16), "wid").astype(jnp.float32),
        lax.psum(up_part.astype(jnp.bfloat16), "wid").astype(jnp.float32),
        lax.psum(grad_part.astype(jnp.bfloat16), "wid").astype(jnp.float32),
    )
    hidden, gate_term, up_term = swiglu_terms(gate, up, hidden_grad)
    total = lax.dot_general(
        gate_term, gate_weight, contract_last, preferred_element_type=jnp.float32
    )
    input_grad = lax.psum_scatter(
        total
        + lax.dot_general(up_term, up_weight, contract_last, preferred_element_type=jnp.float32),
        "hid",
        scatter_dimension=0,
        tiled=True,
    ).astype(jnp.bfloat16)
    contract_first = (((0,), (0,)), ((), ()))
    gate_grad = lax.dot_general(
        all_inputs, gate_term, contract_first, preferred_element_type=jnp.float32
    ).astype(jnp.bfloat16)
    up_grad = lax.dot_general(
        all_inputs, up_term, contract_first, preferred_element_type=jnp.float32
    ).astype(jnp.bfloat16)
    down_grad = lax.dot_general(
        hidden, all_grads, contract_first, preferred_element_type=jnp.float32
    ).astype(jnp.bfloat16)
    return (input_grad, gate_grad, up_grad, down_grad)


def solution(mesh):
    placed = (P("hid", "wid"), P("wid", "hid"), P("wid", "hid"), P("hid", "wid"), P("hid", "wid"))
    return jax.shard_map(
        per_device,
        mesh=mesh,
        in_specs=placed,
        out_specs=(P("hid", "wid"), P("wid", "hid"), P("wid", "hid"), P("hid", "wid")),
        check_vma=False,
    )
```

profile of v0, /device:TPU:8, one launch (start us, length us, event | category | flops | bytes accessed | tf_op | source)
XLA Modules:
  0.0 344.4 jit_solution(14188217543889474345)
XLA Ops:
  7.2 0.0 copy-start
  7.2 0.0 all-gather.5.cloned.1.call-start
  7.2 0.7 all-gather.5.cloned.1.call-update
  7.9 0.0 all-gather.3.cloned.1.call-start
  8.0 0.7 all-gather.3.cloned.1.call-update
  8.7 0.0 all-reduce.3.cloned.1.call-start
  8.7 57.7 %all-gather.5.cloned.1.call-done = bf16[768,1024]{1,0:T(8,128)(2,1)} async-done(((bf16[24,1024]{1,0:T(8,128)(2,1)}), bf16[768,1024]{1,0:T(8,128)(2,1)}) %all-gather.5.cloned.1.call-update) | async-done | bytes 1572880 | tf_op jit(solution)/shard_map/all_gather | solution.py:17
  66.4 4.4 %convolution_convert_fusion.1 = bf16[768,896]{1,0:T(8,128)(2,1)} fusion(bf16[768,1024]{1,0:T(8,128)(2,1)} %all-gather.5.cloned.1.call-done, bf16[1024,896]{1,0:T(8,128)(2,1)S(1)} %copy-done), kind=kOutput, calls=%fused_computation.20 | convolution fusion | flops 1409974272 | bytes 4784128 | tf_op jit(solution)/shard_map/dot_general | solution.py:21
  70.8 0.0 copy-done.7
  70.9 2.9 convolution_convert_fusion.2
  73.7 45.4 %all-gather.3.cloned.1.call-done = bf16[768,1024]{1,0:T(8,128)(2,1)} async-done(((bf16[24,1024]{1,0:T(8,128)(2,1)}), bf16[768,1024]{1,0:T(8,128)(2,1)}) %all-gather.3.cloned.1.call-update) | async-done | bytes 1572880 | tf_op jit(solution)/shard_map/all_gather | solution.py:18
  119.2 4.9 %convolution_convert_fusion.3 = bf16[768,896]{1,0:T(8,128)(2,1)} fusion(bf16[768,1024]{1,0:T(8,128)(2,1)} %all-gather.3.cloned.1.call-done, bf16[896,1024]{1,0:T(8,128)(2,1)} %param.8), kind=kOutput, calls=%fused_computation.22 | convolution fusion | flops 1409974272 | bytes 4784128 | tf_op jit(solution)/shard_map/dot_general | solution.py:23
  124.0 0.0 all-reduce.3.cloned.1.call-update
  124.1 0.2 reduce-scatter.2.cloned.1.call-start
  124.3 104.4 %all-reduce.3.cloned.1.call-done = (bf16[768,896]{1,0:T(8,128)(2,1)}, bf16[768,896]{1,0:T(8,128)(2,1)}, bf16[768,896]{1,0:T(8,128)(2,1)}) async-done(((bf16[768,896]{1,0:T(8,128)(2,1)}, bf16[768,896]{1,0:T(8,128)(2,1)}, bf16[768,896]{1,0:T(8,128)(2,1)}), (bf16[768,896]{1,0:T(8,128)(2,1)}, bf16[768,896]{1,0:T(8,128)(2,1)}, bf16[768,896]{1,0:T(8,128)(2,1)})) %all-reduce.3.cloned.1.call-update) | async-done | bytes 4128784 | tf_op jit(solution)/shard_map/psum | solution.py:28
  228.7 3.4 fusion.2
  232.1 0.0 copy-start.4
  232.1 1.1 copy-done.4
  233.2 1.8 fusion.15
  235.0 0.0 copy-done.2
  235.0 0.0 copy-done.3
  235.0 0.5 copy-done.6
  235.5 3.6 %convolution_add_fusion = f32[768,1024]{1,0:T(8,128)} fusion(f32[768,1024]{1,0:T(8,128)S(1)} %fusion.15, bf16[1024,896]{1,0:T(8,128)(2,1)S(1)} %copy-done.6, bf16[768,896]{1,0:T(8,128)(2,1)S(1)} %copy-done.2, bf16[768,896]{1,0:T(8,128)(2,1)S(1)} %copy-done.3), kind=kOutput, calls=%fused_computation.19 | convolution fusion | flops 1415577600 | bytes 10878976 | tf_op jit(solution)/shard_map/dot_general | solution.py:37
  239.1 0.0 reduce-scatter.2.cloned.1.call-update
  239.1 4.7 %convert_bitcast_fusion.1 = bf16[1024,896]{0,1:T(8,128)(2,1)} fusion(bf16[768,896]{1,0:T(8,128)(2,1)} %copy-done.4, bf16[768,1024]{1,0:T(8,128)(2,1)} %all-gather.5.cloned.1.call-done), kind=kOutput, calls=%fused_computation.17 | convolution fusion | flops 1410203648 | bytes 4784128 | tf_op jit(solution)/shard_map/dot_general | solution.py:43
  243.8 3.8 %copy.9 = bf16[1024,896]{1,0:T(8,128)(2,1)} copy(bf16[1024,896]{0,1:T(8,128)(2,1)} %convert_bitcast_fusion.1) | data formatting | bytes 3670016
  247.6 4.8 %convert_bitcast_fusion = bf16[1024,896]{0,1:T(8,128)(2,1)} fusion(bf16[768,1024]{1,0:T(8,128)(2,1)} %all-gather.5.cloned.1.call-done, bf16[768,896]{1,0:T(8,128)(2,1)S(1)} %copy-done.2, bf16[768,896]{1,0:T(8,128)(2,1)} %get-tuple-element.9), kind=kOutput, calls=%fused_computation.16 | convolution fusion | flops 1415708672 | bytes 6160384 | tf_op jit(solution)/shard_map/dot_general | solution.py:46
  252.4 3.9 %copy.10 = bf16[1024,896]{1,0:T(8,128)(2,1)} copy(bf16[1024,896]{0,1:T(8,128)(2,1)} %convert_bitcast_fusion) | data formatting | bytes 3670016
  256.3 0.0 copy-done.1
  256.3 4.9 %convolution_convert_fusion = bf16[896,1024]{1,0:T(8,128)(2,1)} fusion(bf16[768,1024]{1,0:T(8,128)(2,1)} %all-gather.3.cloned.1.call-done, bf16[768,896]{1,0:T(8,128)(2,1)S(1)} %copy-done.1, bf16[768,896]{1,0:T(8,128)(2,1)} %get-tuple-element.10), kind=kOutput, calls=%fused_computation.18 | convolution fusion | flops 1415708672 | bytes 6160384 | tf_op jit(solution)/shard_map/dot_general | solution.py:49
  261.2 75.1 %reduce-scatter.2.cloned.1.call-done = f32[24,1024]{1,0:T(8,128)} async-done(((f32[768,1024]{1,0:T(8,128)}), f32[24,1024]{1,0:T(8,128)}) %reduce-scatter.2.cloned.1.call-update) | async-done | bytes 98320 | tf_op jit(solution)/shard_map/reduce_scatter | solution.py:35
  336.3 1.5 convert_element_type.53
  (8 shorter events, 0.0 us)
Async XLA Ops:
  7.2 59.3 %copy-start = (bf16[1024,896]{1,0:T(8,128)(2,1)S(1)}, bf16[1024,896]{1,0:T(8,128)(2,1)}, u32[]{:S(2)}) copy-start(bf16[1024,896]{1,0:T(8,128)(2,1)} %param.6) | copy-start | bytes 5505028
  7.2 59.2 %all-gather.5.cloned.1.call-start = ((), (), s32[]{:S(2)}) async-start(), calls=%async_computation.2 | async-start | bytes 1622016 | tf_op jit(solution)/shard_map/all_gather | solution.py:17
  7.9 111.3 %all-gather.3.cloned.1.call-start = ((), (), s32[]{:S(2)}) async-start(), calls=%async_computation.1 | async-start | bytes 1622016 | tf_op jit(solution)/shard_map/all_gather | solution.py:18
  8.7 220.0 %all-reduce.3.cloned.1.call-start = ((), (), s32[]{:S(2)}) async-start(), calls=%async_computation.4 | async-start | bytes 8257536 | tf_op jit(solution)/shard_map/psum | solution.py:28
  66.4 4.4 %copy-start.5 = (bf16[1024,896]{1,0:T(8,128)(2,1)S(1)}, bf16[1024,896]{1,0:T(8,128)(2,1)}, u32[]{:S(2)}) copy-start(bf16[1024,896]{1,0:T(8,128)(2,1)} %param.7) | copy-start | bytes 5505028
  66.4 4.4 %copy-start.7 = (bf16[768,1024]{1,0:T(8,128)(2,1)S(1)}, bf16[768,1024]{1,0:T(8,128)(2,1)}, u32[]{:S(2)}) copy-start(bf16[768,1024]{1,0:T(8,128)(2,1)} %all-gather.5.cloned.1.call-done) | copy-start | bytes 4718596
  124.1 212.3 %reduce-scatter.2.cloned.1.call-start = ((), (), s32[]{:S(2)}) async-start(), calls=%async_computation.3 | async-start | bytes 3244032 | tf_op jit(solution)/shard_map/reduce_scatter | solution.py:35
  232.1 1.1 copy-start.4
  233.2 1.8 copy-start.2
  233.2 1.8 copy-start.3
  233.2 2.3 copy-start.6
  252.4 3.9 %copy-start.1 = (bf16[768,896]{1,0:T(8,128)(2,1)S(1)}, bf16[768,896]{1,0:T(8,128)(2,1)}, u32[]{:S(2)}) copy-start(bf16[768,896]{1,0:T(8,128)(2,1)} %get-tuple-element.8) | copy-start | bytes 4128772
Sparse Core Ops, SparseCore 0:
  10.5 55.8 all-gather.4
  69.0 50.1 all-gather.2
  124.2 104.4 all-reduce.2
  239.2 97.0 reduce-scatter.1
where the time goes:
time: 345 us; the launch traced here: 344 us
  waiting for transfers between devices  284 us (82%)
  matrix products  32 us (9%)
  between operations  13.8 us (4%)
  local copies, waits for them, and re-layouts  9.32 us (3%)
  other arithmetic  4.92 us (1%)
    psum x1, waiting for transfers between devices, per_device(): lax.psum(up_part.astype(jnp.bfloat16), 'wid').astype(jnp.float32)  104 us
    reduce_scatter x1, waiting for transfers between devices, per_device(): lax.psum_scatter(total + lax.dot_general(up_term, up_weight, contract_las...  75.1 us
    all_gather x1, waiting for transfers between devices, per_device(): lax.all_gather(inputs, 'hid', axis=0, tiled=True)  57.7 us
    all_gather x1, waiting for transfers between devices, per_device(): lax.all_gather(out_grad, 'hid', axis=0, tiled=True)  45.4 us
    unnamed x18, local copies, waits for them, and re-layouts  9.32 us
  transfers between devices with their start and end apart: 4, of which 4 were waited for; matrix products, arithmetic and copies ran while one was open for 9% of the time, Pallas kernels for 0%

commit v1 on v0

--- a/solution.py
+++ b/solution.py
@@ -2,6 +2,13 @@
 import jax.numpy as jnp
 from jax import lax
 from jax.sharding import PartitionSpec as P
+
+
+def note_numbers_up(page, chip_axis):
+    return jnp.concatenate(
+        lax.all_to_all(jnp.stack([page for _ in range(lax.axis_size(chip_axis))]), chip_axis, 0, 0),
+        axis=0,
+    )
 
 
 def swiglu_terms(gate, up, hidden_grad):
@@ -15,7 +22,7 @@
 def per_device(inputs, gate_weight, up_weight, down_weight, out_grad):
     all_inputs, all_grads = (
         lax.all_gather(inputs, "hid", axis=0, tiled=True),
-        lax.all_gather(out_grad, "hid", axis=0, tiled=True),
+        note_numbers_up(out_grad, "hid"),
     )
     contract_last = (((1,), (1,)), ((), ()))
     gate_part = jnp.dot(all_inputs, gate_weight, preferred_element_type=jnp.float32)

time: 345 us -> 313 us (0.907)
  waiting for transfers between devices: 284 us -> 239 us
  starting transfers between devices: 0.34 us -> 11.6 us
    all_gather x1 -> x0, waiting for transfers between devices: 45.4 us -> none  [per_device(): lax.all_gather(out_grad, 'hid', axis=0, tiled=True)]
    all_to_all x0 -> x1, waiting for transfers between devices: none -> 40.9 us  [note_numbers_up(): lax.all_to_all(jnp.stack([page for _ in range(lax.axis_size(chip_axis))])...]
    all_gather x1, waiting for transfers between devices: 57.7 us -> 17.8 us  [per_device(): lax.all_gather(inputs, 'hid', axis=0, tiled=True)]
    all_to_all x0 -> x1, starting transfers between devices: none -> 11.3 us  [note_numbers_up(): lax.all_to_all(jnp.stack([page for _ in range(lax.axis_size(chip_axis))])...]
    unnamed x18 -> x16, local copies, waits for them, and re-layouts: 9.32 us -> 9.19 us
where the time goes in v1:
time: 313 us; the launch traced here: 312 us
  waiting for transfers between devices  239 us (76%)
  matrix products  31.8 us (10%)
  between operations  13.8 us (4%)
  starting transfers between devices  11.6 us (4%)
  local copies, waits for them, and re-layouts  11.5 us (4%)
  other arithmetic  4.92 us (2%)
    psum x1, waiting for transfers between devices, per_device(): lax.psum(up_part.astype(jnp.bfloat16), 'wid').astype(jnp.float32)  104 us
    reduce_scatter x1, waiting for transfers between devices, per_device(): lax.psum_scatter(total + lax.dot_general(up_term, up_weight, contract_las...  74.9 us
    all_to_all x1, waiting for transfers between devices, note_numbers_up(): lax.all_to_all(jnp.stack([page for _ in range(lax.axis_size(chip_axis))])...  40.9 us
    all_gather x1, waiting for transfers between devices, per_device(): lax.all_gather(inputs, 'hid', axis=0, tiled=True)  17.8 us
    all_to_all x1, starting transfers between devices, note_numbers_up(): lax.all_to_all(jnp.stack([page for _ in range(lax.axis_size(chip_axis))])...  11.3 us
    unnamed x16, local copies, waits for them, and re-layouts  9.19 us
  transfers between devices with their start and end apart: 4, of which 4 were waited for; matrix products, arithmetic and copies ran while one was open for 9% of the time, Pallas kernels for 0%

profile of v1, /device:TPU:8, one launch (start us, length us, event | category | flops | bytes accessed | tf_op | source)
XLA Modules:
  0.0 312.2 jit_solution(18145956979004753303)
XLA Ops:
  7.2 0.0 copy-start
  7.2 2.3 stack.2
  9.4 11.3 %all-to-all-start = ((bf16[32,24,1024]{2,1,0:T(8,128)(2,1)}), bf16[32,24,1024]{2,1,0:T(8,128)(2,1)S(1)}, u32[]{:S(2)}, u32[]{:S(2)}) async-start(bf16[32,24,1024]{2,1,0:T(8,128)(2,1)} %stack.2), calls=%async_computation | async-start | bytes 3145728 | tf_op jit(solution)/shard_map/all_to_all | solution.py:9
  20.8 0.0 all-gather.2.cloned.1.call-start
  20.8 0.7 all-gather.2.cloned.1.call-update
  21.5 0.0 all-reduce.3.cloned.1.call-start
  21.6 40.9 %all-to-all-done = bf16[32,24,1024]{2,1,0:T(8,128)(2,1)S(1)} async-done(((bf16[32,24,1024]{2,1,0:T(8,128)(2,1)}), bf16[32,24,1024]{2,1,0:T(8,128)(2,1)S(1)}, u32[]{:S(2)}, u32[]{:S(2)}) %all-to-all-start) | async-done | bytes 1572896 | tf_op jit(solution)/shard_map/all_to_all | solution.py:9
  62.4 4.4 %convolution_convert_fusion.3 = bf16[768,896]{1,0:T(8,128)(2,1)} fusion(bf16[768,1024]{1,0:T(8,128)(2,1)S(1)} %bitcast.18, bf16[896,1024]{1,0:T(8,128)(2,1)} %param.8), kind=kOutput, calls=%fused_computation.22 | convolution fusion | flops 1409974272 | bytes 4784128 | tf_op jit(solution)/shard_map/dot_general | solution.py:30
  66.8 17.8 %all-gather.2.cloned.1.call-done = bf16[768,1024]{1,0:T(8,128)(2,1)} async-done(((bf16[24,1024]{1,0:T(8,128)(2,1)}), bf16[768,1024]{1,0:T(8,128)(2,1)}) %all-gather.2.cloned.1.call-update) | async-done | bytes 1572880 | tf_op jit(solution)/shard_map/all_gather | solution.py:24
  84.6 0.0 copy-done
  84.6 4.4 %convolution_convert_fusion.1 = bf16[768,896]{1,0:T(8,128)(2,1)} fusion(bf16[768,1024]{1,0:T(8,128)(2,1)} %all-gather.2.cloned.1.call-done, bf16[1024,896]{1,0:T(8,128)(2,1)S(1)} %copy-done), kind=kOutput, calls=%fused_computation.20 | convolution fusion | flops 1409974272 | bytes 4784128 | tf_op jit(solution)/shard_map/dot_general | solution.py:28
  89.0 0.0 copy-done.4
  89.0 0.0 copy-done.6
  89.0 2.9 convolution_convert_fusion.2
  91.9 0.0 all-reduce.3.cloned.1.call-update
  91.9 0.2 reduce-scatter.2.cloned.1.call-start
  92.2 104.4 %all-reduce.3.cloned.1.call-done = (bf16[768,896]{1,0:T(8,128)(2,1)}, bf16[768,896]{1,0:T(8,128)(2,1)}, bf16[768,896]{1,0:T(8,128)(2,1)}) async-done(((bf16[768,896]{1,0:T(8,128)(2,1)}, bf16[768,896]{1,0:T(8,128)(2,1)}, bf16[768,896]{1,0:T(8,128)(2,1)}), (bf16[768,896]{1,0:T(8,128)(2,1)}, bf16[768,896]{1,0:T(8,128)(2,1)}, bf16[768,896]{1,0:T(8,128)(2,1)})) %all-reduce.3.cloned.1.call-update) | async-done | bytes 4128784 | tf_op jit(solution)/shard_map/psum | solution.py:35
  196.5 3.4 %fusion.2 = bf16[768,896]{1,0:T(8,128)(2,1)S(1)} fusion(bf16[768,896]{1,0:T(8,128)(2,1)} %get-tuple-element.8, bf16[768,896]{1,0:T(8,128)(2,1)} %get-tuple-element.9, bf16[768,896]{1,0:T(8,128)(2,1)} %get-tuple-element.10), kind=kLoop, calls=%fused_computation.8 | loop fusion | flops 8945664 | bytes 5505024 | tf_op jit(solution)/shard_map/convert_element_type | solution.py:18
  199.9 0.0 copy-start.3
  199.9 1.1 copy-done.3
  201.0 1.8 fusion.15
  202.9 0.0 copy-done.1
  202.9 0.5 copy-done.5
  203.4 3.5 %convolution_add_fusion = f32[768,1024]{1,0:T(8,128)} fusion(f32[768,1024]{1,0:T(8,128)S(1)} %fusion.15, bf16[1024,896]{1,0:T(8,128)(2,1)S(1)} %copy-done.5, bf16[768,896]{1,0:T(8,128)(2,1)S(1)} %copy-done.1, bf16[768,896]{1,0:T(8,128)(2,1)S(1)} %copy-done.2), kind=kOutput, calls=%fused_computation.19 | convolution fusion | flops 1415577600 | bytes 10878976 | tf_op jit(solution)/shard_map/dot_general | solution.py:44
  206.9 0.0 reduce-scatter.2.cloned.1.call-update
  206.9 4.7 %convert_bitcast_fusion.1 = bf16[1024,896]{0,1:T(8,128)(2,1)} fusion(bf16[768,896]{1,0:T(8,128)(2,1)} %copy-done.3, bf16[768,1024]{1,0:T(8,128)(2,1)} %all-gather.2.cloned.1.call-done), kind=kOutput, calls=%fused_computation.17 | convolution fusion | flops 1410203648 | bytes 4784128 | tf_op jit(solution)/shard_map/dot_general | solution.py:50
  211.6 3.8 %copy.9 = bf16[1024,896]{1,0:T(8,128)(2,1)} copy(bf16[1024,896]{0,1:T(8,128)(2,1)} %convert_bitcast_fusion.1) | data formatting | bytes 3670016
  215.4 5.2 %convert_bitcast_fusion = bf16[1024,896]{0,1:T(8,128)(2,1)} fusion(bf16[768,1024]{1,0:T(8,128)(2,1)} %all-gather.2.cloned.1.call-done, bf16[768,896]{1,0:T(8,128)(2,1)} %get-tuple-element.10, bf16[768,896]{1,0:T(8,128)(2,1)} %get-tuple-element.9), kind=kOutput, calls=%fused_computation.16 | convolution fusion | flops 1415708672 | bytes 6160384 | tf_op jit(solution)/shard_map/dot_general | solution.py:53
  220.6 3.8 %copy.10 = bf16[1024,896]{1,0:T(8,128)(2,1)} copy(bf16[1024,896]{0,1:T(8,128)(2,1)} %convert_bitcast_fusion) | data formatting | bytes 3670016
  224.4 4.8 %convolution_convert_fusion = bf16[896,1024]{1,0:T(8,128)(2,1)} fusion(bf16[768,1024]{1,0:T(8,128)(2,1)S(1)} %bitcast.19, bf16[768,896]{1,0:T(8,128)(2,1)} %get-tuple-element.8, bf16[768,896]{1,0:T(8,128)(2,1)} %get-tuple-element.10), kind=kOutput, calls=%fused_computation.18 | convolution fusion | flops 1415708672 | bytes 6160384 | tf_op jit(solution)/shard_map/dot_general | solution.py:56
  229.3 74.9 %reduce-scatter.2.cloned.1.call-done = f32[24,1024]{1,0:T(8,128)} async-done(((f32[768,1024]{1,0:T(8,128)}), f32[24,1024]{1,0:T(8,128)}) %reduce-scatter.2.cloned.1.call-update) | async-done | bytes 98320 | tf_op jit(solution)/shard_map/reduce_scatter | solution.py:42
  304.2 1.5 convert_element_type.53
  (6 shorter events, 0.0 us)
Async XLA Ops:
  7.2 77.4 %copy-start = (bf16[1024,896]{1,0:T(8,128)(2,1)S(1)}, bf16[1024,896]{1,0:T(8,128)(2,1)}, u32[]{:S(2)}) copy-start(bf16[1024,896]{1,0:T(8,128)(2,1)} %param.6) | copy-start | bytes 5505028
  9.4 53.0 %all-to-all-start = ((bf16[32,24,1024]{2,1,0:T(8,128)(2,1)}), bf16[32,24,1024]{2,1,0:T(8,128)(2,1)S(1)}, u32[]{:S(2)}, u32[]{:S(2)}) async-start(bf16[32,24,1024]{2,1,0:T(8,128)(2,1)} %stack.2), calls=%async_computation | async-start | bytes 3145728 | tf_op jit(solution)/shard_map/all_to_all | solution.py:9
  20.8 63.8 %all-gather.2.cloned.1.call-start = ((), (), s32[]{:S(2)}) async-start(), calls=%async_computation.2 | async-start | bytes 1622016 | tf_op jit(solution)/shard_map/all_gather | solution.py:24
  21.5 175.0 %all-reduce.3.cloned.1.call-start = ((), (), s32[]{:S(2)}) async-start(), calls=%async_computation.4 | async-start | bytes 8257536 | tf_op jit(solution)/shard_map/psum | solution.py:35
  84.6 4.4 %copy-start.4 = (bf16[1024,896]{1,0:T(8,128)(2,1)S(1)}, bf16[1024,896]{1,0:T(8,128)(2,1)}, u32[]{:S(2)}) copy-start(bf16[1024,896]{1,0:T(8,128)(2,1)} %param.7) | copy-start | bytes 5505028
  84.6 4.4 %copy-start.6 = (bf16[768,1024]{1,0:T(8,128)(2,1)S(1)}, bf16[768,1024]{1,0:T(8,128)(2,1)}, u32[]{:S(2)}) copy-start(bf16[768,1024]{1,0:T(8,128)(2,1)} %all-gather.2.cloned.1.call-done) | copy-start | bytes 4718596
  91.9 212.2 %reduce-scatter.2.cloned.1.call-start = ((), (), s32[]{:S(2)}) async-start(), calls=%async_computation.3 | async-start | bytes 3244032 | tf_op jit(solution)/shard_map/reduce_scatter | solution.py:42
  199.9 1.1 copy-start.3
  201.0 1.8 copy-start.1
  201.0 1.8 copy-start.2
  201.0 2.3 copy-start.5
Sparse Core Ops, SparseCore 0:
  24.1 60.4 all-gather.1
  92.0 104.4 all-reduce.2
  207.0 97.0 reduce-scatter.1
